TPU v7x, 256 devices: a whole 4x4x8 slice. The times are simulated.
256 devices in a mesh: date: 64 (over x, y, z_lo, core), rng: 4 (over z_hi).
Axes of the slice: x: 4, y: 4, z: 8 (z_hi: 4, z_lo: 2; z = z_hi * 2 + z_lo), core: 2. Of those that a mesh axis runs over, the one named last changes fastest.
Arguments:
- slc_re: bfloat16 [64, 2048, 512], P('date', None, 'rng'), may hold values from -170 to 170
- slc_im: bfloat16 [64, 2048, 512], P('date', None, 'rng'), may hold values from -170 to 170
- ref_date: int32 [1], replicated, may hold values from 0 to 63
- gain: float32 [2048], replicated, may hold values from 0.25 to 2
- bperp: int32 [64], replicated, may hold values from -200 to 199
- tdays: int32 [64], replicated, may hold values from 0 to 1899
- mask: int32 [2048, 512], P(None, 'rng'), may hold values from 0 to 1, as said below
Outputs:
- periodogram: float32 [2048, 512, 256], P('date', 'rng')
Inputs may be any that keep to these rules, and one draw needn't show every extreme that they name: `mask`: each aligned block of 32 lines by 128 range columns holds exactly 1024 candidates.
All inputs are finite; a program needn't handle non-finite values.
Results may differ from a plain program's by a relative error of at most 0.0067.
Values may be sent and summed in bfloat16 or wider, within the bound.
No kernel may reach another device: no remote copies, remote signals or barrier semaphores. Data moves between devices by JAX's collectives and lax.ppermute only.
A program may use at most 64 MiB of HBM per device.

v0:
```python
import math
import jax
import jax.numpy as jnp
import numpy as np
from jax import lax
from jax.sharding import PartitionSpec as P

HGRID = 16
VGRID = 16
PHASE_Q = 1024


def dft_table(length):
    split = 64
    hi_count = length // split
    freq = jnp.arange(length, dtype=jnp.int32)[:, None]
    step = 2.0 * math.pi / length
    hi_ang = (freq * (split * jnp.arange(hi_count, dtype=jnp.int32)[None, :]) % length).astype(
        jnp.float32
    ) * step
    lo_ang = (freq * jnp.arange(split, dtype=jnp.int32)[None, :] % length).astype(
        jnp.float32
    ) * step
    hi_c, hi_s = (jnp.cos(hi_ang)[:, :, None], jnp.sin(hi_ang)[:, :, None])
    lo_c, lo_s = (jnp.cos(lo_ang)[:, None, :], jnp.sin(lo_ang)[:, None, :])
    cos_t = (hi_c * lo_c - hi_s * lo_s).reshape(length, length)
    sin_t = (hi_c * lo_s + hi_s * lo_c).reshape(length, length)
    table = jnp.concatenate([cos_t, sin_t], axis=1).astype(jnp.bfloat16)
    return lax.optimization_barrier(table)


def phase_tables(bperp, tdays):
    grid_points = jnp.arange(HGRID * VGRID, dtype=jnp.int32)
    height_step = grid_points // VGRID
    speed_step = grid_points % VGRID
    quanta = (
        bperp[:, None] * height_step[None, :] + tdays[:, None] * speed_step[None, :]
    ) % PHASE_Q
    angles = quanta.astype(jnp.float32) * (2.0 * math.pi / PHASE_Q)
    phase_re = jnp.cos(angles).astype(jnp.bfloat16)
    phase_im = jnp.sin(angles).astype(jnp.bfloat16)
    upper = jnp.concatenate([phase_re, -phase_im], axis=1)
    lower = jnp.concatenate([phase_im, phase_re], axis=1)
    return jnp.concatenate([upper, lower], axis=0)


def shards(slc_re, slc_im, ref_date, gain, bperp, tdays, mask):
    date_dev, lines, rg_dev = slc_re.shape
    assert date_dev == 1
    n_date = lax.axis_size("date")
    n_rng = lax.axis_size("rng")
    cols = rg_dev // n_date
    lines_dev = lines // n_date
    pixel_total = lines * rg_dev * n_rng
    me = lax.axis_index("date")
    f32 = jnp.float32
    own_re = slc_re[0]
    own_im = slc_im[0]
    wide_re = own_re.astype(f32)
    wide_im = own_im.astype(f32)
    local = jnp.sum(wide_re * wide_re + wide_im * wide_im)
    onehot = jnp.where(jnp.arange(n_date) == me, local, 0.0)
    date_sums = lax.psum(onehot, ("date", "rng"))
    scales = lax.rsqrt(date_sums / pixel_total + 1e-06)

    def to_date_rows(x):
        xt = x.T.reshape(cols, n_date, lines).transpose(1, 0, 2).reshape(n_date * cols, lines)
        return lax.all_to_all(xt, "date", split_axis=0, concat_axis=0, tiled=True)

    x_re = to_date_rows(own_re)
    x_im = to_date_rows(own_im)
    ref_index = ref_date[0]
    ref_scale = scales[ref_index]
    ref_re = lax.dynamic_slice_in_dim(x_re, ref_index * cols, cols, 0).astype(f32) * ref_scale
    ref_im = lax.dynamic_slice_in_dim(x_im, ref_index * cols, cols, 0).astype(f32) * ref_scale
    ref_re = jnp.tile(ref_re, (n_date, 1))
    ref_im = jnp.tile(ref_im, (n_date, 1))
    row_scale = jnp.repeat(scales, cols)[:, None]
    a_re = x_re.astype(f32) * row_scale
    a_im = x_im.astype(f32) * row_scale
    ifg_re = (a_re * ref_re + a_im * ref_im).astype(jnp.bfloat16)
    ifg_im = (a_im * ref_re - a_re * ref_im).astype(jnp.bfloat16)
    table = dft_table(lines)
    rows = n_date * cols
    stacked = jnp.concatenate([ifg_re, ifg_im], axis=0)
    fwd = jnp.dot(stacked, table, preferred_element_type=f32)
    spec_re = fwd[:rows, :lines] + fwd[rows:, lines:]
    spec_im = fwd[rows:, :lines] - fwd[:rows, lines:]
    weights = gain[None, :]
    held = jnp.concatenate(
        [(spec_re * weights).astype(jnp.bfloat16), (spec_im * weights).astype(jnp.bfloat16)], axis=0
    )
    back = jnp.dot(held, table, preferred_element_type=f32)
    filt_re = ((back[:rows, :lines] - back[rows:, lines:]) * (1.0 / lines)).astype(jnp.bfloat16)
    filt_im = ((back[:rows, lines:] + back[rows:, :lines]) * (1.0 / lines)).astype(jnp.bfloat16)

    def to_pixel_rows(x):
        got = lax.all_to_all(x.T, "date", split_axis=0, concat_axis=0, tiled=True)
        return got.reshape(n_date, lines_dev, rows).transpose(1, 0, 2).reshape(-1, rows)

    y_re = to_pixel_rows(filt_re)
    y_im = to_pixel_rows(filt_im)
    grid_size = HGRID * VGRID
    phase = phase_tables(bperp, tdays).reshape(2, n_date, 2, grid_size)
    eye = jnp.eye(cols, dtype=jnp.bfloat16)
    big = (phase[:, :, None, None, :, :] * eye[None, None, :, :, None, None]).reshape(
        2 * rows, cols * 2 * grid_size
    )
    ys = jnp.concatenate([y_re, y_im], axis=1)
    spectra = jnp.dot(ys, big, preferred_element_type=f32).reshape(-1, cols, 2, grid_size)
    peri_re = spectra[:, :, 0, :]
    peri_im = spectra[:, :, 1, :]
    wr = y_re.astype(f32)
    wi = y_im.astype(f32)
    sel = jnp.asarray(np.tile(np.eye(cols, dtype=np.float32), (n_date, 1)))
    pixel_power = jnp.dot(wr * wr + wi * wi, sel, precision=lax.Precision.HIGHEST) / n_date
    result = (peri_re * peri_re + peri_im * peri_im) / (n_date * jnp.maximum(pixel_power, 1.0))[
        :, :, None
    ]
    result = result.reshape(lines_dev, n_date, cols, grid_size).transpose(0, 2, 1, 3)
    result = result.reshape(lines_dev, cols * n_date, grid_size)
    mask_rows = lax.dynamic_slice_in_dim(mask, me * lines_dev, lines_dev, 0)
    return result * mask_rows.astype(f32)[:, :, None]


def solution(mesh):
    in_specs = (P("date", None, "rng"), P("date", None, "rng"), P(), P(), P(), P(), P(None, "rng"))
    out_specs = P("date", "rng", None)
    return jax.shard_map(shards, mesh=mesh, in_specs=in_specs, out_specs=out_specs, check_vma=False)
```

profile of v0, /device:TPU:1, one launch (start us, length us, event | category | flops | bytes accessed | tf_op | source)
XLA Modules:
  0.0 211.2 jit_solution(16790087384997871464)
XLA Ops:
  0.0 1.2 copy.24
  1.3 1.3 copy.25
  2.6 10.3 %all-to-all-start.1 = ((bf16[64,2,2048]{2,1,0:T(2,128)(2,1)}), bf16[64,2,2048]{2,1,0:T(2,128)(2,1)S(1)}, u32[]{:S(2)}, u32[]{:S(2)}) async-start(bf16[64,2,2048]{2,1,0:T(2,128)(2,1)} %copy.25), calls=%async_computation.1 | async-start | bytes 1048576 | tf_op jit(solution)/shard_map/all_to_all | solution.py:68
  14.0 2.0 fusion.38
  16.1 1.2 copy.22
  17.3 1.3 copy.23
  18.7 8.2 %subtract_convert_fusion = (bf16[2048,32,64]{0,2,1:T(8,128)(2,1)}, bf16[2048,32,64]{0,2,1:T(8,128)(2,1)}) fusion(f32[2048,64]{0,1:T(8,128)S(1)} %get-tuple-element.19, f32[2048,32]{0,1:T(8,128)S(1)} %get-tuple-element.16, f32[2048,64]{0,1:T(8,128)S(1)} %get-tuple-element.20, f32[2048,32]{0,1:T(8,128)S(1)} %get-tuple-element.15), kind=kLoop, calls=%fused_computation.2 | loop fusion | flops 33554432 | bytes 18350080 | tf_op jit(solution)/shard_map/convert.3
  26.9 8.8 %all-to-all-start = ((bf16[64,2,2048]{2,1,0:T(2,128)(2,1)}), bf16[64,2,2048]{2,1,0:T(2,128)(2,1)S(1)}, u32[]{:S(2)}, u32[]{:S(2)}) async-start(bf16[64,2,2048]{2,1,0:T(2,128)(2,1)} %copy.23), calls=%async_computation | async-start | bytes 1048576 | tf_op jit(solution)/shard_map/all_to_all | solution.py:68
  35.7 13.8 %pad_maximum_fusion = bf16[2048,4096]{0,1:T(8,128)(2,1)} fusion(bf16[2048,2048]{0,1:T(8,128)(2,1)} %bitcast.53, bf16[2048,2048]{0,1:T(8,128)(2,1)} %bitcast.52), kind=kLoop, calls=%fused_computation | loop fusion | flops 33554432 | bytes 33554432 | tf_op jit(solution)/shard_map/concatenate | solution.py:28
  51.7 80.4 %psum.7 = f32[64]{0:T(128)S(1)} all-reduce(f32[64]{0:T(128)S(1)} %compare_select_fusion), channel_id=1, replica_groups=mesh['date'=64,'rng'=4] {'date','rng'}, use_global_device_ids=true, to_apply=%region_1.2 | all-reduce | flops 64 | bytes 512 | tf_op jit(solution)/shard_map/psum | solution.py:63
  136.6 1.7 add_convert_fusion.1
  138.3 10.2 %fusion.11 = f32[256,4096]{1,0:T(8,128)} fusion(bf16[2048,4096]{0,1:T(8,128)(2,1)} %pad_maximum_fusion, bf16[128,2048]{1,0:T(8,128)(2,1)S(1)} %get-tuple-element.10, bf16[128,2048]{1,0:T(8,128)(2,1)S(1)} %get-tuple-element.9), kind=kOutput, calls=%fused_computation.23 | convolution fusion | flops 4297064448 | bytes 22020096 | tf_op jit(solution)/shard_map/dot_general | solution.py:86
  148.5 2.5 %fusion.10 = (bf16[128,2048]{1,0:T(8,128)(2,1)S(1)}, bf16[128,2048]{1,0:T(8,128)(2,1)S(1)}) fusion(f32[256,4096]{1,0:T(8,128)} %fusion.11, f32[2048]{0:T(1024)S(1)} %copy-done.2), kind=kLoop, calls=%fused_computation.22 | loop fusion | flops 1572864 | bytes 5251072 | tf_op jit(solution)/shard_map/convert_element_type | solution.py:91
  151.0 10.2 %fusion.15 = f32[256,4096]{1,0:T(8,128)} fusion(bf16[2048,4096]{0,1:T(8,128)(2,1)} %pad_maximum_fusion, bf16[128,2048]{1,0:T(8,128)(2,1)S(1)} %get-tuple-element.6, bf16[128,2048]{1,0:T(8,128)(2,1)S(1)} %get-tuple-element.5), kind=kOutput, calls=%fused_computation.27 | convolution fusion | flops 4297064448 | bytes 22020096 | tf_op jit(solution)/shard_map/dot_general | solution.py:93
  161.2 2.6 %fusion.30 = (bf16[2048,128]{0,1:T(8,128)(2,1)S(1)}, bf16[2048,128]{0,1:T(8,128)(2,1)S(1)}) fusion(f32[256,4096]{1,0:T(8,128)} %fusion.15), kind=kLoop, calls=%fused_computation.51 | loop fusion | flops 1572864 | bytes 5242880 | tf_op jit(solution)/shard_map/transpose | solution.py:98
  164.8 5.0 %all-to-all-start.3 = ((bf16[64,32,128]{2,1,0:T(8,128)(2,1)}), bf16[64,32,128]{2,1,0:T(8,128)(2,1)S(1)}, u32[]{:S(2)}, u32[]{:S(2)}) async-start(bf16[64,32,128]{2,1,0:T(8,128)(2,1)} %bitcast.17), calls=%async_computation.3 | async-start | bytes 1048576 | tf_op jit(solution)/shard_map/all_to_all | solution.py:98
  170.8 11.9 %all-to-all-done.3 = bf16[64,32,128]{2,1,0:T(8,128)(2,1)S(1)} async-done(((bf16[64,32,128]{2,1,0:T(8,128)(2,1)}), bf16[64,32,128]{2,1,0:T(8,128)(2,1)S(1)}, u32[]{:S(2)}, u32[]{:S(2)}) %all-to-all-start.3) | async-done | bytes 524320 | tf_op jit(solution)/shard_map/all_to_all | solution.py:98
  182.7 4.5 %all-to-all-start.2 = ((bf16[64,32,128]{2,1,0:T(8,128)(2,1)}), bf16[64,32,128]{2,1,0:T(8,128)(2,1)S(1)}, u32[]{:S(2)}, u32[]{:S(2)}) async-start(bf16[64,32,128]{2,1,0:T(8,128)(2,1)} %bitcast.13), calls=%async_computation.2 | async-start | bytes 1048576 | tf_op jit(solution)/shard_map/all_to_all | solution.py:98
  190.0 10.1 %all-to-all-done.2 = bf16[64,32,128]{2,1,0:T(8,128)(2,1)S(1)} async-done(((bf16[64,32,128]{2,1,0:T(8,128)(2,1)}), bf16[64,32,128]{2,1,0:T(8,128)(2,1)S(1)}, u32[]{:S(2)}, u32[]{:S(2)}) %all-to-all-start.2) | async-done | bytes 524320 | tf_op jit(solution)/shard_map/all_to_all | solution.py:98
  200.3 1.3 fusion.19
  201.6 2.6 %fusion = f32[2048,2,1,256]{3,0,2,1:T(8,128)} fusion(f32[2048,2,2,256]{3,0,2,1:T(8,128)S(1)} %fusion.19), kind=kLoop, calls=%fused_computation.4 | loop fusion | flops 3145728 | bytes 12582912 | tf_op jit(solution)/shard_map/add | solution.py:117
  204.2 1.1 fusion.2
  205.4 2.6 %divide_bitcast_fusion = f32[32,2,64,256]{3,2,0,1:T(8,128)S(1)} fusion(f32[32,64,2,256]{3,1,0,2:T(8,128)} %bitcast.54, f32[32,64,2]{1,0,2:T(8,128)S(1)} %div.33), kind=kLoop, calls=%fused_computation.7 | loop fusion | flops 1048576 | bytes 8404992 | tf_op jit(solution)/shard_map/transpose | solution.py:120
  208.5 2.6 %bitcast_multiply_fusion = f32[32,128,256]{2,1,0:T(8,128)} fusion(f32[32,2,64,256]{3,2,1,0:T(8,128)S(1)} %copy.31, f32[32,128]{1,0:T(8,128)S(1)} %dynamic-slice_convert_fusion), kind=kLoop, calls=%fused_computation.6 | loop fusion | flops 1048576 | bytes 8404992 | tf_op jit(solution)/shard_map/mul | solution.py:123
  (45 shorter events, 12.6 us)
Async XLA Ops:
  2.6 24.3 %all-to-all-start.1 = ((bf16[64,2,2048]{2,1,0:T(2,128)(2,1)}), bf16[64,2,2048]{2,1,0:T(2,128)(2,1)S(1)}, u32[]{:S(2)}, u32[]{:S(2)}) async-start(bf16[64,2,2048]{2,1,0:T(2,128)(2,1)} %copy.25), calls=%async_computation.1 | async-start | bytes 1048576 | tf_op jit(solution)/shard_map/all_to_all | solution.py:68
  26.9 106.3 %all-to-all-start = ((bf16[64,2,2048]{2,1,0:T(2,128)(2,1)}), bf16[64,2,2048]{2,1,0:T(2,128)(2,1)S(1)}, u32[]{:S(2)}, u32[]{:S(2)}) async-start(bf16[64,2,2048]{2,1,0:T(2,128)(2,1)} %copy.23), calls=%async_computation | async-start | bytes 1048576 | tf_op jit(solution)/shard_map/all_to_all | solution.py:68
  133.1 0.9 copy-start
  133.4 0.8 copy-start.1
  138.3 10.2 %copy-start.2 = (f32[2048]{0:T(1024)S(1)}, f32[2048]{0:T(1024)}, u32[]{:S(2)}) copy-start(f32[2048]{0:T(1024)} %param.11) | copy-start | bytes 24580
  161.2 26.1 %copy-start.3 = (s32[64]{0:T(128)S(1)}, s32[64]{0:T(128)}, u32[]{:S(2)}) copy-start(s32[64]{0:T(128)} %param.13) | copy-start | bytes 772
  161.2 26.1 %copy-start.4 = (s32[64]{0:T(128)S(1)}, s32[64]{0:T(128)}, u32[]{:S(2)}) copy-start(s32[64]{0:T(128)} %param.12) | copy-start | bytes 772
  164.8 17.9 %all-to-all-start.3 = ((bf16[64,32,128]{2,1,0:T(8,128)(2,1)}), bf16[64,32,128]{2,1,0:T(8,128)(2,1)S(1)}, u32[]{:S(2)}, u32[]{:S(2)}) async-start(bf16[64,32,128]{2,1,0:T(8,128)(2,1)} %bitcast.17), calls=%async_computation.3 | async-start | bytes 1048576 | tf_op jit(solution)/shard_map/all_to_all | solution.py:98
  182.7 17.4 %all-to-all-start.2 = ((bf16[64,32,128]{2,1,0:T(8,128)(2,1)}), bf16[64,32,128]{2,1,0:T(8,128)(2,1)S(1)}, u32[]{:S(2)}, u32[]{:S(2)}) async-start(bf16[64,32,128]{2,1,0:T(8,128)(2,1)} %bitcast.13), calls=%async_computation.2 | async-start | bytes 1048576 | tf_op jit(solution)/shard_map/all_to_all | solution.py:98
  201.6 2.6 %copy-start.5 = (f32[128,2]{1,0:T(8,128)S(1)}, f32[128,2]{1,0:T(8,128)}, u32[]{:S(2)}) copy-start(f32[128,2]{1,0:T(8,128)} %constant.105.clone) | copy-start | bytes 3076
where the time goes:
time: 212 us; the launch traced here: 211 us
  blocking collectives  80.4 us (38%)
  other arithmetic  43.8 us (21%)
  starting transfers between devices  28.7 us (14%)
  matrix products  22.8 us (11%)
  waiting for transfers between devices  22 us (10%)
  local copies, waits for them, and re-layouts  12.6 us (6%)
    psum x1, blocking collectives, shards(): date_sums = lax.psum(onehot, ('date', 'rng'))  80.4 us
    all_to_all x2, waiting for transfers between devices, to_pixel_rows(): got = lax.all_to_all(x.T, 'date', split_axis=0, concat_axis=0, tiled=True)  22 us
    all_to_all x2, starting transfers between devices, to_date_rows(): return lax.all_to_all(xt, 'date', split_axis=0, concat_axis=0, tiled=True)  19.2 us
    concatenate x1, other arithmetic, dft_table(): table = jnp.concatenate([cos_t, sin_t], axis=1).astype(jnp.bfloat16)  13.8 us
    dot_general x1, matrix products, shards(): fwd = jnp.dot(stacked, table, preferred_element_type=f32)  10.2 us
    dot_general x1, matrix products, shards(): back = jnp.dot(held, table, preferred_element_type=f32)  10.2 us
    all_to_all x2, starting transfers between devices, to_pixel_rows(): got = lax.all_to_all(x.T, 'date', split_axis=0, concat_axis=0, tiled=True)  9.56 us
    another operation x1, other arithmetic  8.21 us
  transfers between devices with their start and end apart: 4, of which 2 were waited for; matrix products, arithmetic and copies ran while one was open for 16% of the time, Pallas kernels for 0%

commit v1 on v0

--- a/solution.py
+++ b/solution.py
@@ -60,7 +60,7 @@
     wide_im = own_im.astype(f32)
     local = jnp.sum(wide_re * wide_re + wide_im * wide_im)
     onehot = jnp.where(jnp.arange(n_date) == me, local, 0.0)
-    date_sums = lax.psum(onehot, ("date", "rng"))
+    date_sums = jnp.sum(lax.all_gather(onehot, ("date", "rng")), axis=0)
     scales = lax.rsqrt(date_sums / pixel_total + 1e-06)
 
     def to_date_rows(x):

time: 212 us -> 761 us (3.59)
  blocking collectives: 80.4 us -> 623 us
    all_gather x0 -> x1, blocking collectives: none -> 623 us  [shards(): date_sums = jnp.sum(lax.all_gather(onehot, ('date', 'rng')), axis=0)]
    psum x1 -> x0, blocking collectives: 80.4 us -> none  [shards(): date_sums = lax.psum(onehot, ('date', 'rng'))]
  transfers between devices with their start and end apart: 4 -> 4, of which waited for: 2 -> 2; matrix products, arithmetic and copies ran while one was open for 16% -> 4% of each run, Pallas kernels for 0% -> 0%
where the time goes in v1:
time: 761 us; the launch traced here: 760 us
  blocking collectives  623 us (82%)
  other arithmetic  44.2 us (6%)
  starting transfers between devices  34.6 us (5%)
  matrix products  22.8 us (3%)
  waiting for transfers between devices  22 us (3%)
  local copies, waits for them, and re-layouts  12.6 us (2%)
    all_gather x1, blocking collectives, shards(): date_sums = jnp.sum(lax.all_gather(onehot, ('date', 'rng')), axis=0)  623 us
    all_to_all x2, waiting for transfers between devices, to_pixel_rows(): got = lax.all_to_all(x.T, 'date', split_axis=0, concat_axis=0, tiled=True)  22 us
    all_to_all x2, starting transfers between devices, to_date_rows(): return lax.all_to_all(xt, 'date', split_axis=0, concat_axis=0, tiled=True)  19.2 us
    all_to_all x2, starting transfers between devices, to_pixel_rows(): got = lax.all_to_all(x.T, 'date', split_axis=0, concat_axis=0, tiled=True)  15.4 us
  transfers between devices with their start and end apart: 4, of which 2 were waited for; matrix products, arithmetic and copies ran while one was open for 4% of the time, Pallas kernels for 0%

profile of v1, /device:TPU:1, one launch (start us, length us, event | category | flops | bytes accessed | tf_op | source)
XLA Modules:
  0.0 760.3 jit_solution(3867804300220455670)
XLA Ops:
  0.0 1.2 copy.24
  1.3 1.3 copy.25
  2.6 10.3 %all-to-all-start.1 = ((bf16[64,2,2048]{2,1,0:T(2,128)(2,1)}), bf16[64,2,2048]{2,1,0:T(2,128)(2,1)S(1)}, u32[]{:S(2)}, u32[]{:S(2)}) async-start(bf16[64,2,2048]{2,1,0:T(2,128)(2,1)} %copy.25), calls=%async_computation.1 | async-start | bytes 1048576 | tf_op jit(solution)/shard_map/all_to_all | solution.py:68
  14.0 2.0 fusion.38
  16.1 1.2 copy.22
  17.3 1.3 copy.23
  18.7 8.2 %subtract_convert_fusion = (bf16[2048,32,64]{0,2,1:T(8,128)(2,1)}, bf16[2048,32,64]{0,2,1:T(8,128)(2,1)}) fusion(f32[2048,64]{0,1:T(8,128)S(1)} %get-tuple-element.19, f32[2048,32]{0,1:T(8,128)S(1)} %get-tuple-element.16, f32[2048,64]{0,1:T(8,128)S(1)} %get-tuple-element.20, f32[2048,32]{0,1:T(8,128)S(1)} %get-tuple-element.15), kind=kLoop, calls=%fused_computation.2 | loop fusion | flops 33554432 | bytes 18350080 | tf_op jit(solution)/shard_map/convert.3
  26.9 8.8 %all-to-all-start = ((bf16[64,2,2048]{2,1,0:T(2,128)(2,1)}), bf16[64,2,2048]{2,1,0:T(2,128)(2,1)S(1)}, u32[]{:S(2)}, u32[]{:S(2)}) async-start(bf16[64,2,2048]{2,1,0:T(2,128)(2,1)} %copy.23), calls=%async_computation | async-start | bytes 1048576 | tf_op jit(solution)/shard_map/all_to_all | solution.py:68
  35.7 13.8 %pad_maximum_fusion = bf16[2048,4096]{0,1:T(8,128)(2,1)} fusion(bf16[2048,2048]{0,1:T(8,128)(2,1)} %bitcast.55, bf16[2048,2048]{0,1:T(8,128)(2,1)} %bitcast.54), kind=kLoop, calls=%fused_computation | loop fusion | flops 33554432 | bytes 33554432 | tf_op jit(solution)/shard_map/concatenate | solution.py:28
  51.8 623.3 %all-gather = f32[256,1,64]{2,1,0:T(1,128)S(1)} all-gather(f32[1,1,64]{2,1,0:T(1,128)S(1)} %fusion.50), channel_id=1, replica_groups=mesh['date'=64,'rng'=4] {'date','rng'}, dimensions={0}, use_global_device_ids=true | all-gather | bytes 65792 | tf_op jit(solution)/shard_map/all_gather | solution.py:63
  679.9 1.7 add_convert_fusion.1
  681.6 10.2 %fusion.11 = f32[256,4096]{1,0:T(8,128)} fusion(bf16[2048,4096]{0,1:T(8,128)(2,1)} %pad_maximum_fusion, bf16[128,2048]{1,0:T(8,128)(2,1)S(1)} %get-tuple-element.10, bf16[128,2048]{1,0:T(8,128)(2,1)S(1)} %get-tuple-element.9), kind=kOutput, calls=%fused_computation.23 | convolution fusion | flops 4297064448 | bytes 22020096 | tf_op jit(solution)/shard_map/dot_general | solution.py:86
  691.8 2.5 fusion.10
  694.3 10.2 %fusion.15 = f32[256,4096]{1,0:T(8,128)} fusion(bf16[2048,4096]{0,1:T(8,128)(2,1)} %pad_maximum_fusion, bf16[128,2048]{1,0:T(8,128)(2,1)S(1)} %get-tuple-element.6, bf16[128,2048]{1,0:T(8,128)(2,1)S(1)} %get-tuple-element.5), kind=kOutput, calls=%fused_computation.27 | convolution fusion | flops 4297064448 | bytes 22020096 | tf_op jit(solution)/shard_map/dot_general | solution.py:93
  704.5 2.6 fusion.30
  708.1 10.9 %all-to-all-start.3 = ((bf16[64,32,128]{2,1,0:T(8,128)(2,1)}), bf16[64,32,128]{2,1,0:T(8,128)(2,1)S(1)}, u32[]{:S(2)}, u32[]{:S(2)}) async-start(bf16[64,32,128]{2,1,0:T(8,128)(2,1)} %bitcast.18), calls=%async_computation.3 | async-start | bytes 1048576 | tf_op jit(solution)/shard_map/all_to_all | solution.py:98
  720.0 11.9 %all-to-all-done.3 = bf16[64,32,128]{2,1,0:T(8,128)(2,1)S(1)} async-done(((bf16[64,32,128]{2,1,0:T(8,128)(2,1)}), bf16[64,32,128]{2,1,0:T(8,128)(2,1)S(1)}, u32[]{:S(2)}, u32[]{:S(2)}) %all-to-all-start.3) | async-done | bytes 524320 | tf_op jit(solution)/shard_map/all_to_all | solution.py:98
  731.9 4.5 all-to-all-start.2
  739.2 10.1 %all-to-all-done.2 = bf16[64,32,128]{2,1,0:T(8,128)(2,1)S(1)} async-done(((bf16[64,32,128]{2,1,0:T(8,128)(2,1)}), bf16[64,32,128]{2,1,0:T(8,128)(2,1)S(1)}, u32[]{:S(2)}, u32[]{:S(2)}) %all-to-all-start.2) | async-done | bytes 524320 | tf_op jit(solution)/shard_map/all_to_all | solution.py:98
  749.5 1.3 fusion.19
  750.8 2.6 fusion
  753.3 1.1 fusion.2
  754.6 2.6 divide_bitcast_fusion
  757.7 2.6 bitcast_multiply_fusion
  (46 shorter events, 13.0 us)
Async XLA Ops:
  2.6 24.3 %all-to-all-start.1 = ((bf16[64,2,2048]{2,1,0:T(2,128)(2,1)}), bf16[64,2,2048]{2,1,0:T(2,128)(2,1)S(1)}, u32[]{:S(2)}, u32[]{:S(2)}) async-start(bf16[64,2,2048]{2,1,0:T(2,128)(2,1)} %copy.25), calls=%async_computation.1 | async-start | bytes 1048576 | tf_op jit(solution)/shard_map/all_to_all | solution.py:68
  26.9 649.6 %all-to-all-start = ((bf16[64,2,2048]{2,1,0:T(2,128)(2,1)}), bf16[64,2,2048]{2,1,0:T(2,128)(2,1)S(1)}, u32[]{:S(2)}, u32[]{:S(2)}) async-start(bf16[64,2,2048]{2,1,0:T(2,128)(2,1)} %copy.23), calls=%async_computation | async-start | bytes 1048576 | tf_op jit(solution)/shard_map/all_to_all | solution.py:68
  676.4 0.9 copy-start
  676.7 0.8 copy-start.1
  681.6 10.2 %copy-start.2 = (f32[2048]{0:T(1024)S(1)}, f32[2048]{0:T(1024)}, u32[]{:S(2)}) copy-start(f32[2048]{0:T(1024)} %param.11) | copy-start | bytes 24580
  704.5 31.9 %copy-start.3 = (s32[64]{0:T(128)S(1)}, s32[64]{0:T(128)}, u32[]{:S(2)}) copy-start(s32[64]{0:T(128)} %param.13) | copy-start | bytes 772
  704.5 31.9 %copy-start.4 = (s32[64]{0:T(128)S(1)}, s32[64]{0:T(128)}, u32[]{:S(2)}) copy-start(s32[64]{0:T(128)} %param.12) | copy-start | bytes 772
  708.1 23.7 %all-to-all-start.3 = ((bf16[64,32,128]{2,1,0:T(8,128)(2,1)}), bf16[64,32,128]{2,1,0:T(8,128)(2,1)S(1)}, u32[]{:S(2)}, u32[]{:S(2)}) async-start(bf16[64,32,128]{2,1,0:T(8,128)(2,1)} %bitcast.18), calls=%async_computation.3 | async-start | bytes 1048576 | tf_op jit(solution)/shard_map/all_to_all | solution.py:98
  731.9 17.4 %all-to-all-start.2 = ((bf16[64,32,128]{2,1,0:T(8,128)(2,1)}), bf16[64,32,128]{2,1,0:T(8,128)(2,1)S(1)}, u32[]{:S(2)}, u32[]{:S(2)}) async-start(bf16[64,32,128]{2,1,0:T(8,128)(2,1)} %bitcast.14), calls=%async_computation.2 | async-start | bytes 1048576 | tf_op jit(solution)/shard_map/all_to_all | solution.py:98
  750.8 2.6 copy-start.5
